TPU v7x, 256 devices: a whole 4x4x8 slice. The times are simulated.
256 devices in a mesh: tm: 8 (over y_lo, x), stn: 32 (over y_hi, z, core).
Axes of the slice: x: 4, y: 4 (y_hi: 2, y_lo: 2; y = y_hi * 2 + y_lo), z: 8, core: 2. Of those that a mesh axis runs over, the one named last changes fastest.
Arguments:
- voltages: bfloat16 [1024, 524288], P('stn', 'tm'), may hold values from -6 to 6
- gains: float32 [2, 1024, 256], P(None, 'stn'), may hold values from -4 to 4
Outputs:
- visibility: float32 [256, 2, 1024, 1024], P(('tm', 'stn'))
All inputs are finite; a program needn't handle non-finite values.
Results may differ from a plain program's by a relative error of at most 0.0038.
Values may be sent and summed in bfloat16 or wider, within the bound.
No kernel may reach another device: no remote copies, remote signals or barrier semaphores. Data moves between devices by JAX's collectives and lax.ppermute only.
A program may use at most 128 MiB of HBM per device.

v0:
```python
import numpy as np
import jax
import jax.numpy as jnp
from jax import lax
from jax.sharding import PartitionSpec as P

CHANNELS = 4096
BAND_LOW = 1024
TAPS = 8


def passed_along(x, axis, by):
    devices = lax.axis_size(axis)
    pairs = [(i, i + by) for i in range(devices) if 0 <= i + by < devices]
    return lax.ppermute(x, axis, pairs)


def window_table(chans):
    frame_len = 2 * chans
    total_len = TAPS * frame_len
    positions = np.arange(total_len, dtype=np.float64)
    centred = (positions - (total_len - 1) / 2.0) / frame_len
    taper = np.sin(np.pi * (positions + 0.5) / total_len)
    shaped = np.sinc(centred) * taper * taper
    shaped = shaped / np.sqrt(np.sum(shaped * shaped))
    return shaped.reshape(TAPS, frame_len).astype(np.float32)


def split(x):
    hi = lax.reduce_precision(x, exponent_bits=8, mantissa_bits=7)
    lo = x - hi
    return (hi.astype(jnp.bfloat16), lo.astype(jnp.bfloat16))


def band_tables(frame_len, band):
    half = band // 2
    n_b = 32
    n_a = frame_len // 2 // n_b
    q = jnp.arange(2, dtype=jnp.int32)[:, None, None]
    k = jnp.arange(band, dtype=jnp.int32)[None, None, :]
    chan = 2 * (k % half) + q
    imag_col = k >= half
    a = jnp.arange(n_a, dtype=jnp.int32)[None, :, None]
    b = jnp.arange(n_b, dtype=jnp.int32)[None, :, None]
    p_steps = n_a * 2
    tp = 2.0 * jnp.pi / p_steps * (a * chan % p_steps).astype(jnp.float32)
    tq = 2.0 * jnp.pi / frame_len * (b * (BAND_LOW + chan) % frame_len).astype(jnp.float32)
    pr, pi = (jnp.cos(tp), -jnp.sin(tp))
    qr, qi = (jnp.cos(tq), -jnp.sin(tq))
    b1 = jnp.where(imag_col, qi, qr)
    b2 = jnp.where(imag_col, qr, -qi)
    t = pr[:, :, None, :] * b1[:, None, :, :] + pi[:, :, None, :] * b2[:, None, :, :]
    return split(t.reshape(2, n_a * n_b, band))


def on_device(voltages, gains):
    in_dev, length = voltages.shape
    band = gains.shape[2]
    half_band = band // 2
    frame_len = 2 * CHANNELS
    half_len = frame_len // 2
    frames = length // frame_len
    n_time = lax.axis_size("tm")
    n_station = lax.axis_size("stn")
    all_inputs = in_dev * n_station
    history = TAPS - 1
    slots = frames + history
    window = jnp.asarray(window_table(CHANNELS))
    t_hi, t_lo = band_tables(frame_len, band)
    framed = voltages.reshape(in_dev, frames, frame_len)
    pad = jnp.zeros((in_dev, history, frame_len), voltages.dtype)
    padded = jnp.concatenate([pad, framed, pad], axis=1).astype(jnp.float32)
    windowed = window[0] * padded[:, 0:slots, :]
    for tap_index in range(1, TAPS):
        windowed = windowed + window[tap_index] * padded[:, tap_index : tap_index + slots, :]
    first, second = (windowed[..., :half_len], windowed[..., half_len:])
    folded = jnp.stack([first + second, first - second])
    l_hi, l_lo = split(folded)
    lhs = jnp.stack([l_hi, l_lo], axis=1)
    f32 = jnp.float32
    part_hi = jnp.einsum("qhism,qmk->qhisk", lhs, t_hi, preferred_element_type=f32)
    part_lo = jnp.einsum("qism,qmk->qisk", l_hi, t_lo, preferred_element_type=f32)
    raw = part_hi[:, 0] + part_hi[:, 1] + part_lo
    own = raw[:, :, :frames, :]
    given = passed_along(raw[:, :, frames:, :], "tm", 1)
    own = own.at[:, :, :history, :].add(given)
    own = own.reshape(2, in_dev, frames, 2, half_band)
    raw_re = jnp.transpose(own[:, :, :, 0, :], (3, 0, 1, 2))
    raw_im = jnp.transpose(own[:, :, :, 1, :], (3, 0, 1, 2))
    g = jnp.transpose(gains.reshape(2, in_dev, half_band, 2), (0, 2, 3, 1))[..., None]
    gain_re, gain_im = (g[0], g[1])
    spec_re = gain_re * raw_re - gain_im * raw_im
    spec_im = gain_re * raw_im + gain_im * raw_re
    spectra = jnp.stack([spec_re, spec_im], axis=3).astype(jnp.bfloat16)
    row = in_dev * 2 * frames
    spectra = spectra.reshape(n_time, n_station, row)
    spectra = lax.all_to_all(spectra, "tm", split_axis=0, concat_axis=0, tiled=True)
    spectra = lax.all_to_all(spectra, "stn", split_axis=1, concat_axis=1, tiled=True)
    spectra = spectra.reshape(n_time, n_station, in_dev, 2, frames)
    spectra = jnp.transpose(spectra, (1, 2, 3, 0, 4)).reshape(all_inputs, 2, n_time * frames)
    stacked = spectra.reshape(all_inputs, 2 * n_time * frames)
    flipped = jnp.concatenate([spectra[:, 1], -spectra[:, 0]], axis=-1)
    both = jnp.concatenate([stacked, flipped], axis=0)
    vis = jnp.einsum("ik,jk->ij", both, stacked, preferred_element_type=f32)
    vis = vis * (1.0 / float(n_time * frames))
    return vis.reshape(1, 2, all_inputs, all_inputs)


def solution(mesh):
    in_specs = (P("stn", "tm"), P(None, "stn", None))
    out_specs = P(("tm", "stn"), None, None, None)
    return jax.shard_map(
        on_device, mesh=mesh, in_specs=in_specs, out_specs=out_specs, check_vma=False
    )
```

profile of v0, /device:TPU:1, one launch (start us, length us, event | category | flops | bytes accessed | tf_op | source)
XLA Modules:
  0.0 175.2 jit_solution(2518422193169905856)
XLA Ops:
  0.0 1.0 fusion.43
  1.1 0.3 negate_select_fusion.4
  1.4 1.2 multiply_add_fusion
  2.6 5.4 %reduce-precision_convert_fusion.1 = (bf16[2,4096,256]{2,1,0:T(8,128)(2,1)}, bf16[2,4096,256]{2,1,0:T(8,128)(2,1)}) fusion(f32[2,128,32,256]{3,2,1,0:T(8,128)S(1)} %multiply_add_fusion), kind=kLoop, calls=%fused_computation.26 | loop fusion | flops 8388608 | bytes 16777216 | tf_op jit(solution)/shard_map/convert_element_type | solution.py:32
  8.3 0.4 broadcast_in_dim.15
  8.8 8.0 %maximum_convert_fusion = f32[32,22,8192]{2,0,1:T(8,128)} fusion(bf16[32,7,8192]{2,0,1:T(8,128)(2,1)S(1)} %broadcast_in_dim.15, bf16[32,8,8192]{2,0,1:T(8,128)(2,1)S(1)} %bitcast.87), kind=kLoop, calls=%fused_computation.27 | loop fusion | flops 17301504 | bytes 30932992 | tf_op jit(solution)/shard_map/convert_element_type | solution.py:72
  16.8 50.0 %fusion.1 = f32[32,15,8192]{2,0,1:T(8,128)} fusion(f32[32,22,8192]{2,0,1:T(8,128)} %maximum_convert_fusion, f32[8192]{0:T(1024)S(1)} %copy-done.3, f32[8192]{0:T(1024)S(1)} %copy-done.4, f32[8192]{0:T(1024)S(1)} %copy-done.5, f32[8192]{0:T(1024)S(1)} %copy-done.6, f32[8192]{0:T(1024)S(1)} %copy-done.7, f32[8192]{0:T(1024)S(1)} %copy-done.8, ...), kind=kLoop, calls=%fused_computation.4 | loop fusion | flops 58982400 | bytes 141819904 | tf_op jit(solution)/shard_map/add | solution.py:75
  66.8 13.2 %fusion.19 = (f32[1,1,32,15,4096]{4,2,3,1,0:T(8,128)S(1)}, f32[1,32,15,4096]{3,1,2,0:T(8,128)}, f32[1,32,15,4096]{3,1,2,0:T(8,128)}, f32[1,1,32,15,4096]{4,2,3,1,0:T(8,128)}) fusion(f32[32,15,8192]{2,0,1:T(8,128)} %fusion.1), kind=kLoop, calls=%fused_computation.38 | loop fusion | flops 3932160 | bytes 47185920 | tf_op jit(solution)/shard_map/stack | solution.py:77
  80.0 5.3 %reduce-precision_convert_fusion = (bf16[2,1,32,15,4096]{4,2,3,1,0:T(8,128)(2,1)S(1)}, bf16[2,1,32,15,4096]{4,2,3,1,0:T(8,128)(2,1)S(1)}) fusion(f32[1,1,32,15,4096]{4,2,3,1,0:T(8,128)} %get-tuple-element.22, f32[1,1,32,15,4096]{4,2,3,1,0:T(8,128)S(1)} %get-tuple-element.19), kind=kLoop, calls=%fused_computation.1 | loop fusion | flops 19660800 | bytes 31457280 | tf_op jit(solution)/shard_map/convert_element_type | solution.py:32
  85.4 7.1 %fusion.8 = f32[2,2,32,15,256]{4,2,3,1,0:T(8,128)} fusion(bf16[2,1,32,15,4096]{4,2,3,1,0:T(8,128)(2,1)S(1)} %get-tuple-element.18, bf16[2,1,32,15,4096]{4,2,3,1,0:T(8,128)(2,1)S(1)} %get-tuple-element.17, bf16[2,4096,256]{2,1,0:T(8,128)(2,1)} %get-tuple-element.23), kind=kOutput, calls=%fused_computation.19 | convolution fusion | flops 4034396160 | bytes 21889024 | tf_op jit(solution)/shard_map/qhism,qmk->qhisk/dot_general | solution.py:81
  92.5 7.3 %fusion.22 = f32[2,32,15,256]{3,1,2,0:T(8,128)S(1)} fusion(bf16[2,4096,256]{2,1,0:T(8,128)(2,1)} %get-tuple-element.24, f32[1,32,15,4096]{3,1,2,0:T(8,128)S(1)} %copy-done, f32[1,32,15,4096]{3,1,2,0:T(8,128)} %get-tuple-element.21, f32[2,2,32,15,256]{4,2,3,1,0:T(8,128)} %fusion.8), kind=kOutput, calls=%fused_computation.41 | convolution fusion | flops 2025553920 | bytes 22872064 | tf_op jit(solution)/shard_map/qism,qmk->qisk/dot_general | solution.py:82
  99.8 4.2 %collective-permute-start = (f32[2,32,7,256]{3,1,2,0:T(8,128)S(1)}, f32[2,32,7,256]{3,1,2,0:T(8,128)S(1)}, u32[]{:S(2)}, u32[]{:S(2)}) collective-permute-start(f32[2,32,7,256]{3,1,2,0:T(8,128)S(1)} %slice.160), channel_id=1, source_target_pairs={{0,32},{32,64},{64,96},{96,128},{128,160},{160,192},{192,224},{1,3... | collective-permute-start | bytes 1376264 | tf_op jit(solution)/shard_map/ppermute | solution.py:15
  104.4 8.6 %collective-permute-done = f32[2,32,7,256]{3,1,2,0:T(8,128)S(1)} collective-permute-done((f32[2,32,7,256]{3,1,2,0:T(8,128)S(1)}, f32[2,32,7,256]{3,1,2,0:T(8,128)S(1)}, u32[]{:S(2)}, u32[]{:S(2)}) %collective-permute-start) | collective-permute-done | bytes 458784 | tf_op jit(solution)/shard_map/ppermute | solution.py:15
  113.3 0.6 fusion.57
  113.8 0.3 fusion.40
  114.2 6.7 %copy.31 = bf16[128,2,32,2,8]{4,3,2,1,0:T(2,128)(2,1)} copy(bf16[128,2,32,2,8]{0,4,3,2,1:T(8,128)(2,1)S(1)} %pad_maximum_fusion.1) | data formatting | bytes 524288 | tf_op jit(solution)/shard_map/stack | solution.py:94
  121.0 7.0 %convert_element_type.68 = bf16[8,32,512]{2,1,0:T(8,128)(2,1)S(1)} reshape(bf16[128,2,32,2,8]{4,3,2,1,0:T(2,128)(2,1)} %copy.31) | data formatting | bytes 524288 | tf_op jit(solution)/shard_map/convert_element_type | solution.py:94
  128.0 11.9 %all_to_all.10 = bf16[8,32,512]{2,1,0:T(8,128)(2,1)S(1)} all-to-all(bf16[8,32,512]{2,1,0:T(8,128)(2,1)S(1)} %convert_element_type.68), channel_id=1, replica_groups=mesh['tm'=8,'stn'=32] {'tm'}, dimensions={0} | all-to-all | bytes 524288 | tf_op jit(solution)/shard_map/all_to_all | solution.py:97
  140.1 26.8 %all_to_all.11 = bf16[8,32,512]{2,0,1:T(8,128)(2,1)S(1)} all-to-all(bf16[8,32,512]{2,0,1:T(8,128)(2,1)S(1)} %copy.32), channel_id=1, replica_groups=mesh['tm'=8,'stn'=32] {'stn'}, dimensions={1} | all-to-all | bytes 524288 | tf_op jit(solution)/shard_map/all_to_all | solution.py:98
  166.9 0.5 copy.33
  167.4 0.9 copy.34
  168.3 1.1 reshape_reshape.3
  169.4 1.1 reshape.270
  170.5 4.7 %convolution_multiply_fusion = f32[2048,1024]{1,0:T(8,128)} fusion(bf16[1024,128]{0,1:T(8,128)(2,1)S(1)} %reshape_reshape.3, bf16[1024,64]{0,1:T(8,128)(2,1)S(1)} %get-tuple-element.30, bf16[1024,64]{0,1:T(8,128)(2,1)S(1)} %get-tuple-element.29), kind=kOutput, calls=%fused_computation.33 | convolution fusion | flops 540540928 | bytes 8912896 | tf_op jit(solution)/shard_map/ik,jk->ij/dot_general | solution.py:104
  (37 shorter events, 1.3 us)
Async XLA Ops:
  2.6 5.4 %copy-start.1 = (bf16[32,65536]{1,0:T(8,128)(2,1)S(1)}, bf16[32,65536]{1,0:T(8,128)(2,1)}, u32[]{:S(2)}) copy-start(bf16[32,65536]{1,0:T(8,128)(2,1)} %param.5) | copy-start | bytes 12582916
  8.7 8.1 %copy-start.3 = (f32[8192]{0:T(1024)S(1)}, f32[8192]{0:T(1024)}, u32[]{:S(2)}) copy-start(f32[8192]{0:T(1024)} %constant.101) | copy-start | bytes 98308
  8.7 8.1 %copy-start.4 = (f32[8192]{0:T(1024)S(1)}, f32[8192]{0:T(1024)}, u32[]{:S(2)}) copy-start(f32[8192]{0:T(1024)} %constant.99) | copy-start | bytes 98308
  8.7 8.0 %copy-start.5 = (f32[8192]{0:T(1024)S(1)}, f32[8192]{0:T(1024)}, u32[]{:S(2)}) copy-start(f32[8192]{0:T(1024)} %constant.97) | copy-start | bytes 98308
  8.7 8.0 %copy-start.6 = (f32[8192]{0:T(1024)S(1)}, f32[8192]{0:T(1024)}, u32[]{:S(2)}) copy-start(f32[8192]{0:T(1024)} %constant.95) | copy-start | bytes 98308
  8.7 8.0 %copy-start.7 = (f32[8192]{0:T(1024)S(1)}, f32[8192]{0:T(1024)}, u32[]{:S(2)}) copy-start(f32[8192]{0:T(1024)} %constant.93) | copy-start | bytes 98308
  8.7 8.0 %copy-start.8 = (f32[8192]{0:T(1024)S(1)}, f32[8192]{0:T(1024)}, u32[]{:S(2)}) copy-start(f32[8192]{0:T(1024)} %constant.91) | copy-start | bytes 98308
  8.7 8.0 %copy-start.9 = (f32[8192]{0:T(1024)S(1)}, f32[8192]{0:T(1024)}, u32[]{:S(2)}) copy-start(f32[8192]{0:T(1024)} %constant.89) | copy-start | bytes 98308
  8.8 8.0 %copy-start.10 = (f32[8192]{0:T(1024)S(1)}, f32[8192]{0:T(1024)}, u32[]{:S(2)}) copy-start(f32[8192]{0:T(1024)} %constant.87) | copy-start | bytes 98308
  85.4 7.1 %copy-start = (f32[1,32,15,4096]{3,1,2,0:T(8,128)S(1)}, f32[1,32,15,4096]{3,1,2,0:T(8,128)}, u32[]{:S(2)}) copy-start(f32[1,32,15,4096]{3,1,2,0:T(8,128)} %get-tuple-element.20) | copy-start | bytes 23592964
  92.5 11.6 %copy-start.2 = (f32[2,32,256]{2,1,0:T(8,128)S(1)}, f32[2,32,256]{2,1,0:T(8,128)}, u32[]{:S(2)}) copy-start(f32[2,32,256]{2,1,0:T(8,128)} %param.6) | copy-start | bytes 196612
  99.8 13.1 %collective-permute-start = (f32[2,32,7,256]{3,1,2,0:T(8,128)S(1)}, f32[2,32,7,256]{3,1,2,0:T(8,128)S(1)}, u32[]{:S(2)}, u32[]{:S(2)}) collective-permute-start(f32[2,32,7,256]{3,1,2,0:T(8,128)S(1)} %slice.160), channel_id=1, source_target_pairs={{0,32},{32,64},{64,96},{96,128},{128,160},{160,192},{192,224},{1,3... | collective-permute-start | bytes 1376264 | tf_op jit(solution)/shard_map/ppermute | solution.py:15
where the time goes:
time: 175 us
  other arithmetic  84.9 us (49%)
  blocking collectives  38.7 us (22%)
  local copies, waits for them, and re-layouts  19.4 us (11%)
  matrix products  19 us (11%)
  waiting for transfers between devices  8.58 us (5%)
  starting transfers between devices  4.18 us (2%)
    add x1, other arithmetic, on_device(): windowed + window[tap_index] * padded[:, tap_index:tap_index + slots, :]  50 us
    all_to_all x1, blocking collectives, on_device(): lax.all_to_all(spectra, 'stn', split_axis=1, concat_axis=1, tiled=True)  26.8 us
    another operation x1, other arithmetic, on_device(): folded = jnp.stack([first + second, first - second])  13.2 us
    all_to_all x1, blocking collectives, on_device(): lax.all_to_all(spectra, 'tm', split_axis=0, concat_axis=0, tiled=True)  11.9 us
    convert_element_type x2, other arithmetic, split(): return (hi.astype(jnp.bfloat16), lo.astype(jnp.bfloat16))  10.7 us
    ppermute x1, waiting for transfers between devices, passed_along(): return lax.ppermute(x, axis, pairs)  8.58 us
    convert_element_type x1, other arithmetic, on_device(): padded = jnp.concatenate([pad, framed, pad], axis=1).astype(jnp.float32)  7.96 us
    dot_general x1, matrix products, on_device(): jnp.einsum('qism,qmk->qisk', l_hi, t_lo, preferred_element_type=f32)  7.27 us
  transfers between devices with their start and end apart: 1, of which 1 were waited for; matrix products, arithmetic and copies ran while one was open for 0% of the time, Pallas kernels for 0%

commit v1 on v0

--- a/solution.py
+++ b/solution.py
@@ -7,6 +7,12 @@
 CHANNELS = 4096
 BAND_LOW = 1024
 TAPS = 8
+
+
+def stacked_exchange(value, axis, split, join):
+    pieces = jnp.split(value, lax.axis_size(axis), axis=split)
+    received = lax.all_to_all(jnp.stack(pieces), axis, 0, 0)
+    return jnp.concatenate(received, axis=join)
 
 
 def passed_along(x, axis, by):
@@ -95,7 +101,7 @@
     row = in_dev * 2 * frames
     spectra = spectra.reshape(n_time, n_station, row)
     spectra = lax.all_to_all(spectra, "tm", split_axis=0, concat_axis=0, tiled=True)
-    spectra = lax.all_to_all(spectra, "stn", split_axis=1, concat_axis=1, tiled=True)
+    spectra = stacked_exchange(spectra, "stn", 1, 1)
     spectra = spectra.reshape(n_time, n_station, in_dev, 2, frames)
     spectra = jnp.transpose(spectra, (1, 2, 3, 0, 4)).reshape(all_inputs, 2, n_time * frames)
     stacked = spectra.reshape(all_inputs, 2 * n_time * frames)

time: 175 us -> 176 us (level)
  no operation moved by 1% of the time
where the time goes in v1:
time: 176 us
  other arithmetic  85 us (48%)
  blocking collectives  38.7 us (22%)
  local copies, waits for them, and re-layouts  20 us (11%)
  matrix products  19 us (11%)
  waiting for transfers between devices  8.59 us (5%)
  starting transfers between devices  4.19 us (2%)
    add x1, other arithmetic, on_device(): windowed + window[tap_index] * padded[:, tap_index:tap_index + slots, :]  50 us
    all_to_all x1, blocking collectives, stacked_exchange(): received = lax.all_to_all(jnp.stack(pieces), axis, 0, 0)  26.8 us
    another operation x1, other arithmetic, on_device(): folded = jnp.stack([first + second, first - second])  13.2 us
    all_to_all x1, blocking collectives, on_device(): lax.all_to_all(spectra, 'tm', split_axis=0, concat_axis=0, tiled=True)  11.9 us
    convert_element_type x2, other arithmetic, split(): return (hi.astype(jnp.bfloat16), lo.astype(jnp.bfloat16))  10.7 us
    ppermute x1, waiting for transfers between devices, passed_along(): return lax.ppermute(x, axis, pairs)  8.59 us
    convert_element_type x1, other arithmetic, on_device(): padded = jnp.concatenate([pad, framed, pad], axis=1).astype(jnp.float32)  8.01 us
    dot_general x1, matrix products, on_device(): jnp.einsum('qism,qmk->qisk', l_hi, t_lo, preferred_element_type=f32)  7.27 us
  transfers between devices with their start and end apart: 1, of which 1 were waited for; matrix products, arithmetic and copies ran while one was open for 0% of the time, Pallas kernels for 0%

profile of v1, /device:TPU:1, one launch (start us, length us, event | category | flops | bytes accessed | tf_op | source)
XLA Modules:
  0.0 176.1 jit_solution(2995877657555908953)
XLA Ops:
  0.0 1.0 fusion.47
  1.4 1.2 multiply_add_fusion
  2.6 5.4 %reduce-precision_convert_fusion.1 = (bf16[2,4096,256]{2,1,0:T(8,128)(2,1)}, bf16[2,4096,256]{2,1,0:T(8,128)(2,1)}) fusion(f32[2,128,32,256]{3,2,1,0:T(8,128)S(1)} %multiply_add_fusion), kind=kLoop, calls=%fused_computation.26 | loop fusion | flops 8388608 | bytes 16777216 | tf_op jit(solution)/shard_map/convert_element_type | solution.py:38
  8.3 0.4 broadcast_in_dim.15
  8.8 8.0 %maximum_convert_fusion = f32[32,22,8192]{2,0,1:T(8,128)} fusion(bf16[32,7,8192]{2,0,1:T(8,128)(2,1)S(1)} %broadcast_in_dim.15, bf16[32,8,8192]{2,0,1:T(8,128)(2,1)S(1)} %bitcast.158), kind=kLoop, calls=%fused_computation.27 | loop fusion | flops 17301504 | bytes 30932992 | tf_op jit(solution)/shard_map/convert_element_type | solution.py:78
  16.8 50.0 %fusion.1 = f32[32,15,8192]{2,0,1:T(8,128)} fusion(f32[32,22,8192]{2,0,1:T(8,128)} %maximum_convert_fusion, f32[8192]{0:T(1024)S(1)} %copy-done.3, f32[8192]{0:T(1024)S(1)} %copy-done.4, f32[8192]{0:T(1024)S(1)} %copy-done.5, f32[8192]{0:T(1024)S(1)} %copy-done.6, f32[8192]{0:T(1024)S(1)} %copy-done.7, f32[8192]{0:T(1024)S(1)} %copy-done.8, ...), kind=kLoop, calls=%fused_computation.4 | loop fusion | flops 58982400 | bytes 141819904 | tf_op jit(solution)/shard_map/add | solution.py:81
  66.9 13.2 %fusion.19 = (f32[1,1,32,15,4096]{4,2,3,1,0:T(8,128)S(1)}, f32[1,32,15,4096]{3,1,2,0:T(8,128)}, f32[1,32,15,4096]{3,1,2,0:T(8,128)}, f32[1,1,32,15,4096]{4,2,3,1,0:T(8,128)}) fusion(f32[32,15,8192]{2,0,1:T(8,128)} %fusion.1), kind=kLoop, calls=%fused_computation.38 | loop fusion | flops 3932160 | bytes 47185920 | tf_op jit(solution)/shard_map/stack | solution.py:83
  80.1 5.3 %reduce-precision_convert_fusion = (bf16[2,1,32,15,4096]{4,2,3,1,0:T(8,128)(2,1)S(1)}, bf16[2,1,32,15,4096]{4,2,3,1,0:T(8,128)(2,1)S(1)}) fusion(f32[1,1,32,15,4096]{4,2,3,1,0:T(8,128)} %get-tuple-element.22, f32[1,1,32,15,4096]{4,2,3,1,0:T(8,128)S(1)} %get-tuple-element.19), kind=kLoop, calls=%fused_computation.1 | loop fusion | flops 19660800 | bytes 31457280 | tf_op jit(solution)/shard_map/convert_element_type | solution.py:38
  85.4 7.1 %fusion.8 = f32[2,2,32,15,256]{4,2,3,1,0:T(8,128)} fusion(bf16[2,1,32,15,4096]{4,2,3,1,0:T(8,128)(2,1)S(1)} %get-tuple-element.18, bf16[2,1,32,15,4096]{4,2,3,1,0:T(8,128)(2,1)S(1)} %get-tuple-element.17, bf16[2,4096,256]{2,1,0:T(8,128)(2,1)} %get-tuple-element.23), kind=kOutput, calls=%fused_computation.19 | convolution fusion | flops 4034396160 | bytes 21889024 | tf_op jit(solution)/shard_map/qhism,qmk->qhisk/dot_general | solution.py:87
  92.5 7.3 %fusion.22 = f32[2,32,15,256]{3,1,2,0:T(8,128)S(1)} fusion(bf16[2,4096,256]{2,1,0:T(8,128)(2,1)} %get-tuple-element.24, f32[1,32,15,4096]{3,1,2,0:T(8,128)S(1)} %copy-done, f32[1,32,15,4096]{3,1,2,0:T(8,128)} %get-tuple-element.21, f32[2,2,32,15,256]{4,2,3,1,0:T(8,128)} %fusion.8), kind=kOutput, calls=%fused_computation.41 | convolution fusion | flops 2025553920 | bytes 22872064 | tf_op jit(solution)/shard_map/qism,qmk->qisk/dot_general | solution.py:88
  99.8 4.2 %collective-permute-start = (f32[2,32,7,256]{3,1,2,0:T(8,128)S(1)}, f32[2,32,7,256]{3,1,2,0:T(8,128)S(1)}, u32[]{:S(2)}, u32[]{:S(2)}) collective-permute-start(f32[2,32,7,256]{3,1,2,0:T(8,128)S(1)} %slice.160), channel_id=1, source_target_pairs={{0,32},{32,64},{64,96},{96,128},{128,160},{160,192},{192,224},{1,3... | collective-permute-start | bytes 1376264 | tf_op jit(solution)/shard_map/ppermute | solution.py:21
  104.4 8.6 %collective-permute-done = f32[2,32,7,256]{3,1,2,0:T(8,128)S(1)} collective-permute-done((f32[2,32,7,256]{3,1,2,0:T(8,128)S(1)}, f32[2,32,7,256]{3,1,2,0:T(8,128)S(1)}, u32[]{:S(2)}, u32[]{:S(2)}) %collective-permute-start) | collective-permute-done | bytes 458784 | tf_op jit(solution)/shard_map/ppermute | solution.py:21
  113.3 0.6 fusion.61
  113.9 0.3 fusion.45
  114.3 6.7 %copy.820 = bf16[128,2,32,2,8]{4,3,2,1,0:T(2,128)(2,1)} copy(bf16[128,2,32,2,8]{0,4,3,2,1:T(8,128)(2,1)S(1)} %pad_maximum_fusion.1) | data formatting | bytes 524288 | tf_op jit(solution)/shard_map/stack | solution.py:100
  121.0 7.0 %convert_element_type.68 = bf16[8,32,512]{2,1,0:T(8,128)(2,1)S(1)} reshape(bf16[128,2,32,2,8]{4,3,2,1,0:T(2,128)(2,1)} %copy.820) | data formatting | bytes 524288 | tf_op jit(solution)/shard_map/convert_element_type | solution.py:100
  128.0 11.9 %all_to_all.10 = bf16[8,32,512]{2,1,0:T(8,128)(2,1)S(1)} all-to-all(bf16[8,32,512]{2,1,0:T(8,128)(2,1)S(1)} %convert_element_type.68), channel_id=1, replica_groups=mesh['tm'=8,'stn'=32] {'tm'}, dimensions={0} | all-to-all | bytes 524288 | tf_op jit(solution)/shard_map/all_to_all | solution.py:103
  140.4 0.3 fusion.62
  141.0 26.8 %all_to_all.11 = bf16[32,8,1,512]{3,1,2,0:T(8,128)(2,1)S(1)} all-to-all(bf16[32,8,1,512]{3,1,2,0:T(8,128)(2,1)S(1)} %constant_dynamic-update-slice_fusion), channel_id=1, replica_groups=mesh['tm'=8,'stn'=32] {'stn'}, dimensions={0} | all-to-all | bytes 524288 | tf_op jit(solution)/shard_map/all_to_all | solution.py:14
  167.8 0.5 copy.821
  168.3 0.9 copy.822
  169.2 1.1 reshape_reshape.7
  170.3 1.1 reshape.270
  171.4 4.7 %convolution_multiply_fusion = f32[2048,1024]{1,0:T(8,128)} fusion(bf16[1024,128]{0,1:T(8,128)(2,1)S(1)} %reshape_reshape.7, bf16[1024,64]{0,1:T(8,128)(2,1)S(1)} %get-tuple-element.30, bf16[1024,64]{0,1:T(8,128)(2,1)S(1)} %get-tuple-element.29), kind=kOutput, calls=%fused_computation.33 | convolution fusion | flops 540540928 | bytes 8912896 | tf_op jit(solution)/shard_map/ik,jk->ij/dot_general | solution.py:110
  (70 shorter events, 1.8 us)
Async XLA Ops:
  2.6 5.4 %copy-start.1 = (bf16[32,65536]{1,0:T(8,128)(2,1)S(1)}, bf16[32,65536]{1,0:T(8,128)(2,1)}, u32[]{:S(2)}) copy-start(bf16[32,65536]{1,0:T(8,128)(2,1)} %param.5) | copy-start | bytes 12582916
  8.7 8.1 %copy-start.3 = (f32[8192]{0:T(1024)S(1)}, f32[8192]{0:T(1024)}, u32[]{:S(2)}) copy-start(f32[8192]{0:T(1024)} %constant.101) | copy-start | bytes 98308
  8.7 8.1 %copy-start.4 = (f32[8192]{0:T(1024)S(1)}, f32[8192]{0:T(1024)}, u32[]{:S(2)}) copy-start(f32[8192]{0:T(1024)} %constant.99) | copy-start | bytes 98308
  8.7 8.1 %copy-start.5 = (f32[8192]{0:T(1024)S(1)}, f32[8192]{0:T(1024)}, u32[]{:S(2)}) copy-start(f32[8192]{0:T(1024)} %constant.97) | copy-start | bytes 98308
  8.7 8.1 %copy-start.6 = (f32[8192]{0:T(1024)S(1)}, f32[8192]{0:T(1024)}, u32[]{:S(2)}) copy-start(f32[8192]{0:T(1024)} %constant.95) | copy-start | bytes 98308
  8.7 8.1 %copy-start.7 = (f32[8192]{0:T(1024)S(1)}, f32[8192]{0:T(1024)}, u32[]{:S(2)}) copy-start(f32[8192]{0:T(1024)} %constant.93) | copy-start | bytes 98308
  8.7 8.1 %copy-start.8 = (f32[8192]{0:T(1024)S(1)}, f32[8192]{0:T(1024)}, u32[]{:S(2)}) copy-start(f32[8192]{0:T(1024)} %constant.91) | copy-start | bytes 98308
  8.7 8.1 %copy-start.9 = (f32[8192]{0:T(1024)S(1)}, f32[8192]{0:T(1024)}, u32[]{:S(2)}) copy-start(f32[8192]{0:T(1024)} %constant.89) | copy-start | bytes 98308
  8.8 8.1 %copy-start.10 = (f32[8192]{0:T(1024)S(1)}, f32[8192]{0:T(1024)}, u32[]{:S(2)}) copy-start(f32[8192]{0:T(1024)} %constant.87) | copy-start | bytes 98308
  85.4 7.1 %copy-start = (f32[1,32,15,4096]{3,1,2,0:T(8,128)S(1)}, f32[1,32,15,4096]{3,1,2,0:T(8,128)}, u32[]{:S(2)}) copy-start(f32[1,32,15,4096]{3,1,2,0:T(8,128)} %get-tuple-element.20) | copy-start | bytes 23592964
  92.5 11.6 %copy-start.2 = (f32[2,32,256]{2,1,0:T(8,128)S(1)}, f32[2,32,256]{2,1,0:T(8,128)}, u32[]{:S(2)}) copy-start(f32[2,32,256]{2,1,0:T(8,128)} %param.6) | copy-start | bytes 196612
  99.8 13.1 %collective-permute-start = (f32[2,32,7,256]{3,1,2,0:T(8,128)S(1)}, f32[2,32,7,256]{3,1,2,0:T(8,128)S(1)}, u32[]{:S(2)}, u32[]{:S(2)}) collective-permute-start(f32[2,32,7,256]{3,1,2,0:T(8,128)S(1)} %slice.160), channel_id=1, source_target_pairs={{0,32},{32,64},{64,96},{96,128},{128,160},{160,192},{192,224},{1,3... | collective-permute-start | bytes 1376264 | tf_op jit(solution)/shard_map/ppermute | solution.py:21
